TPU v7x, 32 devices: a whole 2x2x4 slice. The times are simulated.
32 devices in a mesh: tm: 2 (over x), state: 16 (over z, y, core).
Axes of the slice: x: 2, y: 2, z: 4, core: 2. Of those that a mesh axis runs over, the one named last changes fastest.
Arguments:
- anomalies: bfloat16 [4, 24576, 256], P('tm', 'state'), may hold values from -23 to 23, as said below
- obs_weight: float32 [4, 24576], P('tm', 'state'), may hold values from 0.05 to 6, as said below
Outputs:
- smoothed: bfloat16 [4, 24576, 256], P('tm', 'state')
- suffix: float32 [4, 256, 256], P('tm')
Inputs may be any that keep to these rules, and one draw needn't show every extreme that they name: Member anomalies of order one, with member columns correlated. `obs_weight`: positive weights.
All inputs are finite; a program needn't handle non-finite values. Where the computation divides by a largest or mean magnitude, that divisor is 1e-20 or more.
Results may differ from a plain program's by a relative error of at most 0.001.
The roundings to bfloat16 on the way count: a program that leaves them out, or rounds other values in their place, can miss the bound.
Values sent between devices are 32-bit elements; how exact they have to be, the bound alone decides.
No kernel may reach another device: no remote copies, remote signals or barrier semaphores. Data moves between devices by JAX's collectives and lax.ppermute only.
A program may use at most 64 MiB of HBM per device.

v0:
```python
import jax
import jax.numpy as jnp
from jax import lax
from jax.sharding import PartitionSpec as P

NS_STEPS = 4


def carried_in(value, axis, join, neutral):
    count, mine = (lax.axis_size(axis), lax.axis_index(axis))
    pieces = lax.all_gather(value, axis)
    pieces = pieces[::-1]
    mine = count - 1 - mine
    so_far = jnp.full_like(value, 0) + jnp.asarray(neutral, value.dtype)

    def hop(position, so_far):
        longer = join(so_far, pieces[position])
        return jnp.where(position < mine, longer, so_far)

    return lax.fori_loop(0, count - 1, hop, so_far)


def newton_root(covariance):
    identity = jnp.eye(covariance.shape[-1], dtype=jnp.float32)
    row_bound = jnp.max(jnp.sum(jnp.abs(covariance), axis=-1), axis=-1)
    iterate = covariance / row_bound[:, None, None]
    inverse_root = jnp.broadcast_to(identity, covariance.shape)
    for sweep_index in range(NS_STEPS):
        factor = 1.5 * identity - 0.5 * jnp.matmul(
            inverse_root, iterate, precision=lax.Precision.HIGHEST
        )
        iterate = jnp.matmul(iterate, factor, precision=lax.Precision.HIGHEST)
        inverse_root = jnp.matmul(factor, inverse_root, precision=lax.Precision.HIGHEST)
    return inverse_root / jnp.sqrt(row_bound)[:, None, None]


def combine(earlier, later):
    return jnp.matmul(later, earlier, precision=lax.Precision.HIGHEST)


def on_device(anomalies, obs_weight):
    times_dev, rows_dev, members = anomalies.shape
    total_rows = rows_dev * lax.axis_size("state")
    weighted = (anomalies * obs_weight[:, :, None]).astype(jnp.bfloat16)
    partial_gram = jnp.einsum(
        "trm,trn->tmn", weighted, weighted, preferred_element_type=jnp.float32
    )
    gram_sum = lax.psum(partial_gram, "state")
    covariance = gram_sum / total_rows + jnp.eye(members, dtype=jnp.float32)
    transform = newton_root(covariance)
    local_product = transform[times_dev - 1]
    time_index = 0
    local_product = jnp.matmul(
        transform[time_index], local_product, precision=lax.Precision.HIGHEST
    )
    identity = jnp.eye(members, dtype=jnp.float32)
    remote = carried_in(local_product, "tm", combine, identity)
    product = remote
    suffixes = []
    for time_index in range(times_dev - 1, -1, -1):
        product = jnp.matmul(transform[time_index], product, precision=lax.Precision.HIGHEST)
        suffixes.append(product)
    suffix = jnp.stack(suffixes[::-1])
    smoothed = jnp.einsum(
        "trm,tmn->trn", anomalies, suffix.astype(jnp.bfloat16), preferred_element_type=jnp.float32
    ).astype(jnp.bfloat16)
    return (smoothed, suffix)


def solution(mesh):
    placed = (P("tm", "state", None), P("tm", "state"))
    return jax.shard_map(
        on_device,
        mesh=mesh,
        in_specs=placed,
        out_specs=(P("tm", "state", None), P("tm", None, None)),
        check_vma=False,
    )
```

profile of v0, /device:TPU:0, one launch (start us, length us, event | category | flops | bytes accessed | tf_op | source)
XLA Modules:
  0.0 135.0 jit_solution(14095974973290434030)
XLA Ops:
  7.2 0.0 all-reduce.2.cloned.1.call-start
  7.2 4.3 %fusion.1 = f32[2,256,256]{2,1,0:T(8,128)} fusion(bf16[2,1536,256]{2,1,0:T(8,128)(2,1)} %param.2, f32[2,1536]{1,0:T(2,128)} %param.3), kind=kOutput, calls=%fused_computation.3 | convolution fusion | flops 405012480 | bytes 2109440 | tf_op jit(solution)/shard_map/trm,trn->tmn/dot_general | solution.py:45
  11.5 0.0 all-reduce.2.cloned.1.call-update
  11.6 93.2 %all-reduce.2.cloned.1.call-done = f32[2,256,256]{2,1,0:T(8,128)} async-done(((f32[2,256,256]{2,1,0:T(8,128)}), f32[2,256,256]{2,1,0:T(8,128)}) %all-reduce.2.cloned.1.call-update) | async-done | bytes 524304 | tf_op jit(solution)/shard_map/psum | solution.py:48
  104.9 1.2 abs_reduce_fusion
  106.1 0.1 reduce_max.9
  106.2 0.0 copy-start.2
  106.2 1.8 %fusion.6 = f32[2,256,256]{2,1,0:T(8,128)S(1)} fusion(f32[256,256]{1,0:T(8,128)S(1)} %fusion.13, f32[256,256]{1,0:T(8,128)S(1)} %fusion.14, f32[2,256,256]{2,1,0:T(8,128)} %all-reduce.2.cloned.1.call-done, f32[2]{0:T(128)S(1)} %reduce_max.9), kind=kOutput, calls=%fused_computation.13 | convolution fusion | flops 403308544 | bytes 1572872 | tf_op jit(solution)/shard_map/dot_general | solution.py:29
  108.0 0.6 fusion.10
  108.7 0.0 copy-done.2
  108.7 0.7 fusion.17
  109.4 0.7 fusion.5
  110.1 0.7 fusion.23
  110.7 0.7 fusion.22
  111.4 0.7 fusion.4
  112.1 0.7 fusion.24
  112.7 0.7 fusion.25
  113.4 0.7 fusion.3
  114.0 0.7 convolution_divide_fusion
  114.7 0.4 fusion.15
  115.1 9.4 %all-gather = f32[512,256]{1,0:T(8,128)S(1)} all-gather(f32[256,256]{1,0:T(8,128)S(1)} %fusion.15), channel_id=2, replica_groups=mesh['tm'=2,'state'=16] {'tm'}, dimensions={0}, use_global_device_ids=true | all-gather | bytes 786432 | tf_op jit(solution)/shard_map/all_gather | solution.py:11
  124.4 0.0 copy-start.1
  124.4 0.3 convolution_select_fusion
  124.7 0.4 fusion.16
  125.1 0.4 convolution_bitcast_fusion
  125.6 0.3 copy-done.1
  125.9 0.0 copy-start
  125.9 0.7 fusion
  126.5 0.1 copy-done
  126.6 1.6 %copy.9 = bf16[2,1536,256]{2,1,0:T(8,128)(2,1)} copy(bf16[2,1536,256]{1,2,0:T(8,128)(2,1)S(1)} %fusion) | data formatting | bytes 3145728
  (4 shorter events, 0.1 us)
Async XLA Ops:
  7.2 97.7 %all-reduce.2.cloned.1.call-start = ((), (), s32[]{:S(2)}) async-start(), calls=%async_computation | async-start | bytes 1048576 | tf_op jit(solution)/shard_map/psum | solution.py:48
  106.2 2.5 %copy-start.2 = (f32[2,256,256]{2,1,0:T(8,128)S(1)}, f32[2,256,256]{2,1,0:T(8,128)}, u32[]{:S(2)}) copy-start(f32[2,256,256]{2,1,0:T(8,128)} %all-reduce.2.cloned.1.call-done) | copy-start | bytes 1572868
  124.4 1.4 %copy-start.1 = (bf16[2,1536,256]{2,1,0:T(8,128)(2,1)S(1)}, bf16[2,1536,256]{2,1,0:T(8,128)(2,1)}, u32[]{:S(2)}) copy-start(bf16[2,1536,256]{2,1,0:T(8,128)(2,1)} %param.2) | copy-start | bytes 4718596
  125.9 0.8 copy-start
Sparse Core Ops, SparseCore 0:
  12.0 92.8 all-reduce.1
where the time goes:
time: 135 us
  waiting for transfers between devices  93.3 us (69%)
  matrix products  14.8 us (11%)
  between operations  14.2 us (11%)
  blocking collectives  9.35 us (7%)
  local copies, waits for them, and re-layouts  1.98 us (1%)
  other arithmetic  1.4 us (1%)
    psum x1, waiting for transfers between devices, on_device(): gram_sum = lax.psum(partial_gram, 'state')  93.2 us
    all_gather x1, blocking collectives, carried_in(): pieces = lax.all_gather(value, axis)  9.35 us
    dot_general x1, matrix products, on_device(): jnp.einsum('trm,trn->tmn', weighted, weighted, preferred_element_type=jnp...  4.31 us
    dot_general x4, matrix products, newton_root(): jnp.matmul(inverse_root, iterate, precision=lax.Precision.HIGHEST)  3.79 us
  transfers between devices with their start and end apart: 1, of which 1 were waited for; matrix products, arithmetic and copies ran while one was open for 0% of the time, Pallas kernels for 0%

commit v1 on v0

--- a/solution.py
+++ b/solution.py
@@ -45,7 +45,7 @@
     partial_gram = jnp.einsum(
         "trm,trn->tmn", weighted, weighted, preferred_element_type=jnp.float32
     )
-    gram_sum = lax.psum(partial_gram, "state")
+    gram_sum = jnp.sum(lax.all_gather(partial_gram, "state"), axis=0)
     covariance = gram_sum / total_rows + jnp.eye(members, dtype=jnp.float32)
     transform = newton_root(covariance)
     local_product = transform[times_dev - 1]

time: 135 us -> 121 us (0.90)
  waiting for transfers between devices: 93.3 us -> 77.7 us
  other arithmetic: 1.4 us -> 4.34 us
    psum x1 -> x0, waiting for transfers between devices: 93.2 us -> none  [on_device(): gram_sum = lax.psum(partial_gram, 'state')]
    all_gather x0 -> x1, waiting for transfers between devices: none -> 77.7 us  [on_device(): gram_sum = jnp.sum(lax.all_gather(partial_gram, 'state'), axis=0)]
    reduce_sum x0 -> x1, other arithmetic: none -> 3.98 us  [on_device(): gram_sum = jnp.sum(lax.all_gather(partial_gram, 'state'), axis=0)]
where the time goes in v1:
time: 121 us
  waiting for transfers between devices  77.7 us (64%)
  between operations  14.2 us (12%)
  matrix products  13.7 us (11%)
  blocking collectives  9.15 us (8%)
  other arithmetic  4.34 us (4%)
  local copies, waits for them, and re-layouts  1.98 us (2%)
    all_gather x1, waiting for transfers between devices, on_device(): gram_sum = jnp.sum(lax.all_gather(partial_gram, 'state'), axis=0)  77.7 us
    all_gather x1, blocking collectives, carried_in(): pieces = lax.all_gather(value, axis)  9.15 us
    dot_general x1, matrix products, on_device(): jnp.einsum('trm,trn->tmn', weighted, weighted, preferred_element_type=jnp...  4.32 us
    reduce_sum x1, other arithmetic, on_device(): gram_sum = jnp.sum(lax.all_gather(partial_gram, 'state'), axis=0)  3.98 us
    dot_general x4, matrix products, newton_root(): jnp.matmul(inverse_root, iterate, precision=lax.Precision.HIGHEST)  2.68 us
    dot_general x4, matrix products, newton_root(): jnp.matmul(factor, inverse_root, precision=lax.Precision.HIGHEST)  2.59 us
  transfers between devices with their start and end apart: 1, of which 1 were waited for; matrix products, arithmetic and copies ran while one was open for 0% of the time, Pallas kernels for 0%

profile of v1, /device:TPU:0, one launch (start us, length us, event | category | flops | bytes accessed | tf_op | source)
XLA Modules:
  0.0 121.1 jit_solution(1492839329790061692)
XLA Ops:
  7.2 0.0 all-gather.4.cloned.1.call-start
  7.2 4.3 %fusion.1 = f32[2,256,256]{2,1,0:T(8,128)} fusion(bf16[2,1536,256]{2,1,0:T(8,128)(2,1)} %param.2, f32[2,1536]{1,0:T(2,128)} %param.3), kind=kOutput, calls=%fused_computation.3 | convolution fusion | flops 405012480 | bytes 2109440 | tf_op jit(solution)/shard_map/trm,trn->tmn/dot_general | solution.py:45
  11.5 0.0 all-gather.4.cloned.1.call-update
  11.6 77.7 %all-gather.4.cloned.1.call-done = f32[32,256,256]{2,1,0:T(8,128)} async-done(((f32[2,256,256]{2,1,0:T(8,128)}), f32[32,256,256]{2,1,0:T(8,128)}) %all-gather.4.cloned.1.call-update) | async-done | bytes 8388624 | tf_op jit(solution)/shard_map/all_gather | solution.py:48
  89.3 4.0 %reduce_sum.18 = f32[2,256,256]{2,1,0:T(8,128)S(1)} reduce(f32[16,2,256,256]{3,2,1,0:T(8,128)} %bitcast.35, f32[]{:T(128)} %constant.10.clone.1), dimensions={0}, to_apply=%region_0.0 | reduce | flops 1966080 | bytes 8912900 | tf_op jit(solution)/shard_map/reduce_sum | solution.py:48
  93.3 0.2 abs_reduce_fusion
  93.5 0.1 reduce_max.9
  93.6 0.7 fusion.6
  94.3 0.7 fusion.17
  95.0 0.6 fusion.10
  95.7 0.7 fusion.5
  96.3 0.7 fusion.23
  97.0 0.7 fusion.22
  97.7 0.7 fusion.4
  98.3 0.7 fusion.25
  99.0 0.7 fusion.24
  99.7 0.7 fusion.3
  100.3 0.7 convolution_divide_fusion
  101.0 0.4 fusion.15
  101.4 9.2 %all-gather.1 = f32[512,256]{1,0:T(8,128)S(1)} all-gather(f32[256,256]{1,0:T(8,128)S(1)} %fusion.15), channel_id=3, replica_groups=mesh['tm'=2,'state'=16] {'tm'}, dimensions={0}, use_global_device_ids=true | all-gather | bytes 786432 | tf_op jit(solution)/shard_map/all_gather | solution.py:11
  110.5 0.0 copy-start.1
  110.5 0.3 convolution_select_fusion
  110.8 0.4 fusion.16
  111.2 0.4 convolution_bitcast_fusion
  111.6 0.3 copy-done.1
  111.9 0.0 copy-start
  111.9 0.7 fusion
  112.6 0.1 copy-done
  112.7 1.6 %copy.12 = bf16[2,1536,256]{2,1,0:T(8,128)(2,1)} copy(bf16[2,1536,256]{1,2,0:T(8,128)(2,1)S(1)} %fusion) | data formatting | bytes 3145728
  (4 shorter events, 0.1 us)
Async XLA Ops:
  7.2 82.1 %all-gather.4.cloned.1.call-start = ((), (), s32[]{:S(2)}) async-start(), calls=%async_computation | async-start | bytes 8912896 | tf_op jit(solution)/shard_map/all_gather | solution.py:48
  110.5 1.4 %copy-start.1 = (bf16[2,1536,256]{2,1,0:T(8,128)(2,1)S(1)}, bf16[2,1536,256]{2,1,0:T(8,128)(2,1)}, u32[]{:S(2)}) copy-start(bf16[2,1536,256]{2,1,0:T(8,128)(2,1)} %param.2) | copy-start | bytes 4718596
  111.9 0.8 copy-start
Sparse Core Ops, SparseCore 0:
  11.7 77.5 all-gather.3
